TPU v7x, 512 devices: a whole 4x8x8 slice. The times are simulated.
512 devices in a mesh: blk: 64 (over y, z_lo, core), head: 8 (over z_hi, x).
Axes of the slice: x: 4, y: 8, z: 8 (z_hi: 2, z_lo: 4; z = z_hi * 4 + z_lo), core: 2. Of those that a mesh axis runs over, the one named last changes fastest.
Arguments:
- query_rows: bfloat16 [16384, 5120], P(('blk', 'head')), may hold values from -12 to 12
- key_rows: bfloat16 [16384, 1024], P(('blk', 'head')), may hold values from -6 to 6
- value_rows: bfloat16 [16384, 1024], P(('blk', 'head')), may hold values from -6 to 6
- out_grads: bfloat16 [16384, 5120], P(('blk', 'head')), may hold values from -1.75 to 1.75
- lengths: int32 [128], replicated, may hold values from 1 to 128, as said below
- ancestors: int32 [128, 5], replicated, may hold values from -1 to 126, as said below
Outputs:
- query_grads: bfloat16 [16384, 5120], P(('blk', 'head'))
- key_grads: bfloat16 [16384, 1024], P(('blk', 'head'))
- value_grads: bfloat16 [16384, 1024], P(('blk', 'head'))
Inputs may be any that keep to these rules, and one draw needn't show every extreme that they name: `ancestors`: row t lists, in increasing order and followed by -1 entries, the tiles above tile t in the trie other than the 1 prompt tiles, which form a chain above every other tile. Every listed tile is a non-prompt tile below t that lies on the device of tile t or on one of the 2 devices before it; the last listed tile is the parent of t, and the row of a listed tile is a prefix of row t. Rows of prompt tiles are all -1. Some row has no -1 entry. On the devices before the last 3, the last tile of each device not a multiple of 3 has as parent the last tile of the device before, and the second-to-last tile of each device d >= 2 with d % 3 != 1 has as parent the second-to-last tile of the device before; those of the other devices have no non-prompt ancestor. lengths[t] slots of tile t hold tokens, the rest is padding; tile 0 is full.
All inputs are finite; a program needn't handle non-finite values.
Results may differ from a plain program's by a relative error of at most 0.0052.
Values may be sent and summed in bfloat16 or wider, within the bound.
No kernel may reach another device: no remote copies, remote signals or barrier semaphores. Data moves between devices by JAX's collectives and lax.ppermute only.
A program may use at most 64 MiB of HBM per device.

v0:
```python
import jax
import jax.numpy as jnp
from jax import lax
from jax.sharding import PartitionSpec as P

HD = 128
TILE = 128
SPAN_DEV = 2
PROMPT_TILES = 1
ANC = 5
KEYT = 7


def spread(value, axis, source):
    kept = jnp.where(lax.axis_index(axis) == source, value, 0).astype(value.dtype)
    return lax.psum(kept, axis)


def passed_along(block, axis, distance):
    devices = range(lax.axis_size(axis))
    route = [(i - distance, i) for i in devices if i - distance in devices]
    return lax.ppermute(block, axis, route)


def visible_mask(tile_id, tile_ids, listed, lengths):
    position = jnp.arange(TILE, dtype=jnp.int32)
    slot_ok = jnp.concatenate(
        [jnp.arange(PROMPT_TILES, dtype=jnp.int32) < tile_id, listed >= 0, jnp.ones((1,), bool)]
    )
    key_len = jnp.take(lengths, jnp.maximum(tile_ids, 0))
    key_ok = slot_ok[:, None] & (position[None, :] < key_len[:, None])
    own_slot = jnp.arange(KEYT) == KEYT - 1
    causal = position[None, None, :] <= position[:, None, None]
    allowed = key_ok[None, :, :] & (causal | ~own_slot[None, :, None])
    return allowed.reshape(TILE, KEYT * TILE)


def tile_backward(queries, grads_out, key_block, value_block, allowed, live_rows, scaling):
    scores = (
        jnp.einsum("igrd,jgd->grij", queries, key_block, preferred_element_type=jnp.float32)
        * scaling
    )
    scores = jnp.where(allowed, scores, -jnp.inf)
    row_max = jnp.max(scores, axis=-1, keepdims=True)
    log_total = row_max + jnp.log(jnp.sum(jnp.exp(scores - row_max), axis=-1, keepdims=True))
    weights = jnp.where(allowed & live_rows[:, None], jnp.exp(scores - log_total), 0.0)
    weight_grads = jnp.einsum(
        "igrd,jgd->grij", grads_out, value_block, preferred_element_type=jnp.float32
    )
    row_dot = jnp.sum(weights * weight_grads, axis=-1, keepdims=True)
    score_grads = (weights * (weight_grads - row_dot)).astype(jnp.bfloat16)
    weights_low = weights.astype(jnp.bfloat16)
    query_part = (
        jnp.einsum("grij,jgd->igrd", score_grads, key_block, preferred_element_type=jnp.float32)
        * scaling
    )
    key_part = jnp.einsum(
        "grij,igrd->jgd", score_grads, queries, preferred_element_type=jnp.float32
    )
    value_part = jnp.einsum(
        "grij,igrd->jgd", weights_low, grads_out, preferred_element_type=jnp.float32
    )
    return (query_part.astype(jnp.bfloat16), key_part, value_part)


def shards(query_rows, key_rows, value_rows, out_grads, lengths, ancestors):
    head_query, head_key, head_value, head_grad = (
        lax.all_to_all(query_rows, "head", split_axis=1, concat_axis=0, tiled=True),
        lax.all_to_all(key_rows, "head", split_axis=1, concat_axis=0, tiled=True),
        lax.all_to_all(value_rows, "head", split_axis=1, concat_axis=0, tiled=True),
        lax.all_to_all(out_grads, "head", split_axis=1, concat_axis=0, tiled=True),
    )
    row_count = head_query.shape[0]
    tiles_here = row_count // TILE
    kv_width = head_key.shape[1]
    kv_heads = kv_width // HD
    group_size = head_query.shape[1] // kv_width
    scaling = HD ** (-0.5)
    block_index = lax.axis_index("blk")
    first_tile = block_index * tiles_here
    window_first = (block_index - SPAN_DEV) * tiles_here
    window_slots = (SPAN_DEV + 1) * tiles_here
    own_states = jnp.concatenate(
        [
            head_key.reshape(tiles_here, TILE, kv_width),
            head_value.reshape(tiles_here, TILE, kv_width),
        ],
        axis=2,
    )
    my_lists = lax.dynamic_slice_in_dim(ancestors, first_tile, tiles_here, 0)
    prompt_ids = jnp.arange(PROMPT_TILES, dtype=jnp.int32)
    pieces = [spread(own_states[:PROMPT_TILES], "blk", 0)]
    for offset in range(SPAN_DEV, 0, -1):
        pieces.append(passed_along(own_states, "blk", offset))
    pieces.append(own_states)
    table = jnp.concatenate(pieces, axis=0)
    slot_index = jnp.arange(window_slots, dtype=jnp.int32)
    prompt_sum = jnp.zeros((PROMPT_TILES, TILE, 2 * kv_width), jnp.float32)
    near_sum = jnp.zeros((window_slots, TILE * 2 * kv_width), jnp.float32)
    query_parts = []
    for local in range(tiles_here):
        tile_id = first_tile + local
        listed = my_lists[local]
        tile_ids = jnp.concatenate([prompt_ids, listed, tile_id[None]])
        near_rows = jnp.where(listed >= 0, PROMPT_TILES + listed - window_first, 0)
        own_row = jnp.full((1,), PROMPT_TILES + SPAN_DEV * tiles_here + local, jnp.int32)
        table_rows = jnp.concatenate([prompt_ids, near_rows, own_row])
        chosen = jnp.take(table, table_rows, axis=0)
        key_block = chosen[:, :, :kv_width].reshape(KEYT * TILE, kv_heads, HD)
        value_block = chosen[:, :, kv_width:].reshape(KEYT * TILE, kv_heads, HD)
        allowed = visible_mask(tile_id, tile_ids, listed, lengths)
        live_rows = jnp.arange(TILE, dtype=jnp.int32) < lengths[tile_id]
        tile_query = head_query[local * TILE : (local + 1) * TILE].reshape(
            TILE, kv_heads, group_size, HD
        )
        tile_grad = head_grad[local * TILE : (local + 1) * TILE].reshape(
            TILE, kv_heads, group_size, HD
        )
        query_part, key_part, value_part = tile_backward(
            tile_query, tile_grad, key_block, value_block, allowed, live_rows, scaling
        )
        query_parts.append(query_part.reshape(TILE, group_size * kv_width))
        tile_terms = jnp.concatenate(
            [key_part.reshape(KEYT, TILE, kv_width), value_part.reshape(KEYT, TILE, kv_width)],
            axis=2,
        )
        prompt_sum = prompt_sum + tile_terms[:PROMPT_TILES]
        window_ids = jnp.concatenate(
            [listed - window_first, jnp.full((1,), SPAN_DEV * tiles_here + local, jnp.int32)]
        )
        usable = jnp.concatenate([listed >= 0, jnp.ones((1,), bool)])
        placing = ((window_ids[:, None] == slot_index[None, :]) & usable[:, None]).astype(
            jnp.float32
        )
        near_sum = near_sum + jnp.einsum(
            "sw,sx->wx",
            placing,
            tile_terms[PROMPT_TILES:].reshape(ANC + 1, TILE * 2 * kv_width),
            precision=lax.Precision.HIGHEST,
        )
    root_total = lax.psum(prompt_sum, "blk")
    near_parts = near_sum.reshape(SPAN_DEV + 1, tiles_here, TILE, 2 * kv_width)
    total = near_parts[SPAN_DEV]
    for offset in range(1, SPAN_DEV + 1):
        total = total + passed_along(near_parts[SPAN_DEV - offset], "blk", -offset)
    total = total.at[:PROMPT_TILES].add(jnp.where(block_index == 0, root_total, 0.0))
    key_out = (total[:, :, :kv_width] * scaling).astype(jnp.bfloat16).reshape(row_count, kv_width)
    value_out = total[:, :, kv_width:].astype(jnp.bfloat16).reshape(row_count, kv_width)
    query_out = jnp.concatenate(query_parts, axis=0)
    query_grads, key_grads, value_grads = (
        lax.all_to_all(query_out, "head", split_axis=0, concat_axis=1, tiled=True),
        lax.all_to_all(key_out, "head", split_axis=0, concat_axis=1, tiled=True),
        lax.all_to_all(value_out, "head", split_axis=0, concat_axis=1, tiled=True),
    )
    return (query_grads, key_grads, value_grads)


def solution(mesh):
    placed = (
        P(("blk", "head"), None),
        P(("blk", "head"), None),
        P(("blk", "head"), None),
        P(("blk", "head"), None),
        P(),
        P(),
    )
    return jax.shard_map(
        shards,
        mesh=mesh,
        in_specs=placed,
        out_specs=(P(("blk", "head"), None), P(("blk", "head"), None), P(("blk", "head"), None)),
        check_vma=False,
    )
```

profile of v0, /device:TPU:2, one launch (start us, length us, event | category | flops | bytes accessed | tf_op | source)
XLA Modules:
  0.0 1101.3 jit_solution(1257224561000166744)
XLA Ops:
  7.2 0.8 copy-done
  8.0 0.6 copy_bitcast_fusion.7
  8.7 13.3 %all-to-all-start = ((bf16[32,8,128]{2,0,1:T(8,128)(2,1)}), bf16[32,8,128]{2,0,1:T(8,128)(2,1)S(1)}, u32[]{:S(2)}, u32[]{:S(2)}) async-start(bf16[32,8,128]{2,0,1:T(8,128)(2,1)} %copy_bitcast_fusion.7), calls=%async_computation | async-start | bytes 131072 | tf_op jit(solution)/shard_map/all_to_all | solution.py:69
  21.9 0.8 constant_dynamic-slice_fusion
  23.3 1.4 fusion.74
  24.7 1.3 gather_fusion.3
  26.1 1.3 gather_fusion.1
  27.5 1.5 copy_bitcast_fusion.6
  29.0 1.3 iota_compare_fusion.3
  30.7 9.6 all-to-all-start.1
  40.4 1.7 copy.149
  42.1 0.7 copy.148
  42.9 0.4 broadcast_and_fusion.1
  43.3 5.8 all-to-all-done.1
  49.1 4.8 all-to-all-start.2
  53.9 3.6 collective-permute-start
  57.5 1.3 collective-permute-start.1
  58.8 0.6 fusion.43
  59.6 472.7 %all-reduce.3.cloned.1.call-done = bf16[1,128,256]{2,1,0:T(8,128)(2,1)} async-done(((bf16[1,128,256]{2,1,0:T(8,128)(2,1)}), bf16[1,128,256]{2,1,0:T(8,128)(2,1)}) %all-reduce.3.cloned.1.call-update) | async-done | bytes 65552 | tf_op jit(solution)/shard_map/psum | solution.py:16
  532.2 0.9 maximum_maximum_fusion
  533.1 0.6 gather_fusion.2
  533.7 0.6 gather_fusion
  534.5 10.4 all-to-all-start.3
  545.2 0.2 reshape.357
  545.4 9.0 all-to-all-done.3
  554.4 0.2 reshape.359
  554.6 0.5 fusion.6
  555.1 0.5 exponential_reduce_fusion.1
  555.6 0.7 fusion.14
  556.4 1.0 fusion.3
  557.3 0.7 fusion.10
  558.1 0.4 fusion.8
  558.5 0.5 fusion.38
  559.6 0.5 copy.110
  560.1 0.5 fusion.7
  560.6 0.5 exponential_reduce_fusion
  561.1 0.7 fusion.12
  561.8 0.9 fusion
  562.8 0.7 fusion.11
  563.5 0.5 fusion.31
  564.0 0.5 copy.111
  564.5 0.8 fusion.45
  565.3 0.8 convolution_add_fusion
  566.1 0.3 fusion.69
  566.5 1.3 collective-permute-start.2
  567.8 1.3 collective-permute-start.3
  569.1 0.4 fusion.9
  569.6 0.7 fusion.26
  570.3 8.4 collective-permute-done.3
  578.8 1.1 fusion.24
  579.9 465.2 %all-reduce.5.cloned.1.call-done = f32[1,128,256]{2,1,0:T(8,128)} async-done(((f32[1,128,256]{2,1,0:T(8,128)}), f32[1,128,256]{2,1,0:T(8,128)}) %all-reduce.5.cloned.1.call-update) | async-done | bytes 131088 | tf_op jit(solution)/shard_map/psum | solution.py:141
  1045.1 0.9 fusion.27
  1046.1 0.6 slice.174
  1046.7 10.3 all-to-all-start.6
  1057.0 0.6 fusion.25
  1057.7 8.2 all-to-all-done.6
  1065.8 4.7 all-to-all-start.5
  1070.6 0.8 pad_maximum_fusion
  1071.3 8.1 all-to-all-done.5
  1079.4 4.8 all-to-all-start.4
  1084.2 0.6 copy_bitcast_fusion.4
  1084.8 0.6 copy_bitcast_fusion.5
  1085.4 8.3 all-to-all-done.4
  1093.7 0.8 copy.107
  (54 shorter events, 2.8 us)
Async XLA Ops:
  7.2 0.8 copy-start
  8.0 34.1 %copy-start.1 = (bf16[32,5120]{1,0:T(8,128)(2,1)S(1)}, bf16[32,5120]{1,0:T(8,128)(2,1)}, u32[]{:S(2)}) copy-start(bf16[32,5120]{1,0:T(8,128)(2,1)} %param.15) | copy-start | bytes 983044
  8.7 22.1 %all-to-all-start = ((bf16[32,8,128]{2,0,1:T(8,128)(2,1)}), bf16[32,8,128]{2,0,1:T(8,128)(2,1)S(1)}, u32[]{:S(2)}, u32[]{:S(2)}) async-start(bf16[32,8,128]{2,0,1:T(8,128)(2,1)} %copy_bitcast_fusion.7), calls=%async_computation | async-start | bytes 131072 | tf_op jit(solution)/shard_map/all_to_all | solution.py:69
  30.7 18.4 %all-to-all-start.1 = ((bf16[32,8,128]{2,0,1:T(8,128)(2,1)}), bf16[32,8,128]{2,0,1:T(8,128)(2,1)S(1)}, u32[]{:S(2)}, u32[]{:S(2)}) async-start(bf16[32,8,128]{2,0,1:T(8,128)(2,1)} %copy_bitcast_fusion.6), calls=%async_computation.1 | async-start | bytes 131072 | tf_op jit(solution)/shard_map/all_to_all | solution.py:70
  49.1 485.4 %all-to-all-start.2 = ((bf16[32,8,640]{2,0,1:T(8,128)(2,1)}), bf16[32,8,640]{2,0,1:T(8,128)(2,1)S(1)}, u32[]{:S(2)}, u32[]{:S(2)}) async-start(bf16[32,8,640]{2,0,1:T(8,128)(2,1)} %bitcast.235), calls=%async_computation.2 | async-start | bytes 655360 | tf_op jit(solution)/shard_map/all_to_all | solution.py:68
  53.9 478.3 %all-reduce.3.cloned.1.call-start = ((), (), s32[]{:S(2)}) async-start(), calls=%async_computation.7 | async-start | bytes 131072 | tf_op jit(solution)/shard_map/psum | solution.py:16
  53.9 478.3 %collective-permute-start = (bf16[2,128,256]{2,1,0:T(8,128)(2,1)S(1)}, bf16[2,128,256]{2,1,0:T(8,128)(2,1)S(1)}, u32[]{:S(2)}, u32[]{:S(2)}) collective-permute-start(bf16[2,128,256]{2,1,0:T(8,128)(2,1)S(1)} %pad_maximum_fusion.1), channel_id=1, source_target_pairs={{0,16},{8,24},{16,32},{24,40},{32,48},{40,56},{48,64},{56,72},{64,... | collective-permute-start | bytes 393224 | tf_op jit(solution)/shard_map/ppermute | solution.py:22
  57.5 474.7 %collective-permute-start.1 = (bf16[2,128,256]{2,1,0:T(8,128)(2,1)S(1)}, bf16[2,128,256]{2,1,0:T(8,128)(2,1)S(1)}, u32[]{:S(2)}, u32[]{:S(2)}) collective-permute-start(bf16[2,128,256]{2,1,0:T(8,128)(2,1)S(1)} %pad_maximum_fusion.1), channel_id=1, source_target_pairs={{0,8},{8,16},{16,24},{24,32},{32,40},{40,48},{48,56},{56,64},{64,7... | collective-permute-start | bytes 393224 | tf_op jit(solution)/shard_map/ppermute | solution.py:22
  534.5 19.9 %all-to-all-start.3 = ((bf16[32,8,640]{2,0,1:T(8,128)(2,1)}), bf16[32,8,640]{2,0,1:T(8,128)(2,1)S(1)}, u32[]{:S(2)}, u32[]{:S(2)}) async-start(bf16[32,8,640]{2,0,1:T(8,128)(2,1)} %bitcast.234), calls=%async_computation.3 | async-start | bytes 655360 | tf_op jit(solution)/shard_map/all_to_all | solution.py:71
  544.9 500.2 %all-reduce.5.cloned.1.call-start = ((), (), s32[]{:S(2)}) async-start(), calls=%async_computation.8 | async-start | bytes 262144 | tf_op jit(solution)/shard_map/psum | solution.py:141
  566.5 3.9 collective-permute-start.2
  567.8 11.0 %collective-permute-start.3 = (f32[2,128,256]{2,1,0:T(8,128)S(1)}, f32[2,128,256]{2,1,0:T(8,128)}, u32[]{:S(2)}, u32[]{:S(2)}) collective-permute-start(f32[2,128,256]{2,1,0:T(8,128)S(1)} %bitcast.269), channel_id=1, source_target_pairs={{16,0},{24,8},{32,16},{40,24},{48,32},{56,40},{64,48},{72,56},{80,... | collective-permute-start | bytes 786440 | tf_op jit(solution)/shard_map/ppermute | solution.py:22
  1046.7 19.1 %all-to-all-start.6 = ((bf16[8,32,128]{2,1,0:T(8,128)(2,1)}), bf16[8,32,128]{2,1,0:T(8,128)(2,1)S(1)}, u32[]{:S(2)}, u32[]{:S(2)}) async-start(bf16[8,32,128]{2,1,0:T(8,128)(2,1)} %bitcast.69), calls=%async_computation.6 | async-start | bytes 131072 | tf_op jit(solution)/shard_map/all_to_all | solution.py:153
  1065.8 13.6 %all-to-all-start.5 = ((bf16[8,32,128]{2,1,0:T(8,128)(2,1)}), bf16[8,32,128]{2,1,0:T(8,128)(2,1)S(1)}, u32[]{:S(2)}, u32[]{:S(2)}) async-start(bf16[8,32,128]{2,1,0:T(8,128)(2,1)} %bitcast.67), calls=%async_computation.5 | async-start | bytes 131072 | tf_op jit(solution)/shard_map/all_to_all | solution.py:152
  1079.4 14.3 %all-to-all-start.4 = ((bf16[8,32,640]{2,1,0:T(8,128)(2,1)}), bf16[8,32,640]{2,1,0:T(8,128)(2,1)S(1)}, u32[]{:S(2)}, u32[]{:S(2)}) async-start(bf16[8,32,640]{2,1,0:T(8,128)(2,1)} %bitcast.43), calls=%async_computation.4 | async-start | bytes 655360 | tf_op jit(solution)/shard_map/all_to_all | solution.py:151
Sparse Core Ops, SparseCore 0:
  59.6 472.5 all-reduce.2
  570.5 474.6 all-reduce.4
where the time goes:
time: 1100 us
  waiting for transfers between devices  986 us (90%)
  starting transfers between devices  65.3 us (6%)
  local copies, waits for them, and re-layouts  17.1 us (2%)
  between operations  14.5 us (1%)
  other arithmetic  11 us (1%)
    psum x1, waiting for transfers between devices, spread(): return lax.psum(kept, axis)  473 us
    psum x1, waiting for transfers between devices, shards(): root_total = lax.psum(prompt_sum, 'blk')  465 us
  transfers between devices with their start and end apart: 13, of which 9 were waited for; matrix products, arithmetic and copies ran while one was open for 2% of the time, Pallas kernels for 0%

commit v1 on v0

--- a/solution.py
+++ b/solution.py
@@ -13,7 +13,7 @@
 
 def spread(value, axis, source):
     kept = jnp.where(lax.axis_index(axis) == source, value, 0).astype(value.dtype)
-    return lax.psum(kept, axis)
+    return jnp.sum(lax.all_gather(kept, axis), 0)
 
 
 def passed_along(block, axis, distance):

time: 1100 us -> 725 us (0.66)
  waiting for transfers between devices: 986 us -> 618 us
    psum x1 -> x0, waiting for transfers between devices: 473 us -> none  [spread(): return lax.psum(kept, axis)]
    all_gather x0 -> x1, waiting for transfers between devices: none -> 87.4 us  [spread(): return jnp.sum(lax.all_gather(kept, axis), 0)]
  transfers between devices with their start and end apart: 13 -> 13, of which waited for: 9 -> 10; matrix products, arithmetic and copies ran while one was open for 2% -> 3% of each run, Pallas kernels for 0% -> 0%
where the time goes in v1:
time: 725 us; the launch traced here: 724 us
  waiting for transfers between devices  618 us (85%)
  starting transfers between devices  56.2 us (8%)
  local copies, waits for them, and re-layouts  14.9 us (2%)
  between operations  14.5 us (2%)
  other arithmetic  12.9 us (2%)
  matrix products  7.66 us (1%)
    psum x1, waiting for transfers between devices, shards(): root_total = lax.psum(prompt_sum, 'blk')  468 us
    all_gather x1, waiting for transfers between devices, spread(): return jnp.sum(lax.all_gather(kept, axis), 0)  87.4 us
  transfers between devices with their start and end apart: 13, of which 10 were waited for; matrix products, arithmetic and copies ran while one was open for 3% of the time, Pallas kernels for 0%

profile of v1, /device:TPU:2, one launch (start us, length us, event | category | flops | bytes accessed | tf_op | source)
XLA Modules:
  0.0 724.0 jit_solution(4226015968503339106)
XLA Ops:
  7.2 0.8 copy-done
  8.0 0.6 copy_bitcast_fusion.7
  8.7 13.3 %all-to-all-start = ((bf16[32,8,128]{2,0,1:T(8,128)(2,1)}), bf16[32,8,128]{2,0,1:T(8,128)(2,1)S(1)}, u32[]{:S(2)}, u32[]{:S(2)}) async-start(bf16[32,8,128]{2,0,1:T(8,128)(2,1)} %copy_bitcast_fusion.7), calls=%async_computation | async-start | bytes 131072 | tf_op jit(solution)/shard_map/all_to_all | solution.py:69
  21.9 1.5 copy_bitcast_fusion.6
  23.4 7.3 %all-to-all-done = bf16[32,8,128]{2,0,1:T(8,128)(2,1)S(1)} async-done(((bf16[32,8,128]{2,0,1:T(8,128)(2,1)}), bf16[32,8,128]{2,0,1:T(8,128)(2,1)S(1)}, u32[]{:S(2)}, u32[]{:S(2)}) %all-to-all-start) | async-done | bytes 65568 | tf_op jit(solution)/shard_map/all_to_all | solution.py:69
  30.7 4.7 all-to-all-start.1
  35.5 8.8 %all-to-all-done.1 = bf16[32,8,128]{2,0,1:T(8,128)(2,1)S(1)} async-done(((bf16[32,8,128]{2,0,1:T(8,128)(2,1)}), bf16[32,8,128]{2,0,1:T(8,128)(2,1)S(1)}, u32[]{:S(2)}, u32[]{:S(2)}) %all-to-all-start.1) | async-done | bytes 65568 | tf_op jit(solution)/shard_map/all_to_all | solution.py:70
  44.3 0.6 fusion.43
  45.0 1.7 copy.149
  46.7 4.8 all-to-all-start.2
  51.5 0.8 constant_dynamic-slice_fusion
  52.5 0.6 gather_fusion.3
  53.2 0.6 gather_fusion.1
  53.8 0.6 fusion.74
  54.7 1.2 iota_compare_fusion.3
  56.4 0.7 copy.148
  57.2 0.4 broadcast_and_fusion.1
  57.8 3.3 all-to-all-done.2
  61.1 6.4 all-to-all-start.3
  67.5 3.4 collective-permute-start
  70.9 1.3 collective-permute-start.1
  72.7 8.2 %all-to-all-done.3 = bf16[32,8,640]{2,0,1:T(8,128)(2,1)S(1)} async-done(((bf16[32,8,640]{2,0,1:T(8,128)(2,1)}), bf16[32,8,640]{2,0,1:T(8,128)(2,1)S(1)}, u32[]{:S(2)}, u32[]{:S(2)}) %all-to-all-start.3) | async-done | bytes 327712 | tf_op jit(solution)/shard_map/all_to_all | solution.py:71
  81.4 87.4 %all-gather.3.cloned.1.call-done = bf16[64,128,256]{2,1,0:T(8,128)(2,1)} async-done(((bf16[1,128,256]{2,1,0:T(8,128)(2,1)}), bf16[64,128,256]{2,1,0:T(8,128)(2,1)}) %all-gather.3.cloned.1.call-update) | async-done | bytes 4194320 | tf_op jit(solution)/shard_map/all_gather | solution.py:16
  168.8 2.8 reduce.10
  171.6 0.6 gather_fusion
  172.4 0.5 fusion.6
  172.9 0.5 exponential_reduce_fusion.1
  173.4 0.7 fusion.14
  174.1 1.0 fusion.3
  175.1 0.7 fusion.10
  175.8 0.4 fusion.8
  176.3 0.5 fusion.38
  176.7 0.6 gather_fusion.2
  177.8 0.5 copy.110
  178.3 0.5 fusion.7
  178.7 0.5 exponential_reduce_fusion
  179.3 0.7 fusion.12
  180.0 0.9 fusion
  180.9 0.7 fusion.11
  181.7 0.5 fusion.31
  182.2 0.5 copy.111
  182.7 0.8 fusion.45
  183.5 0.8 convolution_add_fusion
  184.3 0.3 fusion.69
  184.7 1.3 collective-permute-start.2
  186.0 1.3 collective-permute-start.3
  187.3 0.4 fusion.9
  187.8 0.7 fusion.26
  188.5 9.9 %collective-permute-done.3 = f32[2,128,256]{2,1,0:T(8,128)} collective-permute-done((f32[2,128,256]{2,1,0:T(8,128)S(1)}, f32[2,128,256]{2,1,0:T(8,128)}, u32[]{:S(2)}, u32[]{:S(2)}) %collective-permute-start.3) | collective-permute-done | bytes 262176 | tf_op jit(solution)/shard_map/ppermute | solution.py:22
  198.5 1.1 fusion.24
  199.5 468.3 %all-reduce.2.cloned.1.call-done = f32[1,128,256]{2,1,0:T(8,128)} async-done(((f32[1,128,256]{2,1,0:T(8,128)}), f32[1,128,256]{2,1,0:T(8,128)}) %all-reduce.2.cloned.1.call-update) | async-done | bytes 131088 | tf_op jit(solution)/shard_map/psum | solution.py:141
  667.8 0.9 fusion.27
  668.8 0.6 slice.174
  669.4 10.3 %all-to-all-start.6 = ((bf16[8,32,128]{2,1,0:T(8,128)(2,1)}), bf16[8,32,128]{2,1,0:T(8,128)(2,1)S(1)}, u32[]{:S(2)}, u32[]{:S(2)}) async-start(bf16[8,32,128]{2,1,0:T(8,128)(2,1)} %bitcast.70), calls=%async_computation.6 | async-start | bytes 131072 | tf_op jit(solution)/shard_map/all_to_all | solution.py:153
  679.8 0.6 fusion.25
  680.4 8.2 %all-to-all-done.6 = bf16[8,32,128]{2,1,0:T(8,128)(2,1)S(1)} async-done(((bf16[8,32,128]{2,1,0:T(8,128)(2,1)}), bf16[8,32,128]{2,1,0:T(8,128)(2,1)S(1)}, u32[]{:S(2)}, u32[]{:S(2)}) %all-to-all-start.6) | async-done | bytes 65568 | tf_op jit(solution)/shard_map/all_to_all | solution.py:153
  688.6 4.7 all-to-all-start.5
  693.3 0.8 pad_maximum_fusion
  694.0 8.1 %all-to-all-done.5 = bf16[8,32,128]{2,1,0:T(8,128)(2,1)S(1)} async-done(((bf16[8,32,128]{2,1,0:T(8,128)(2,1)}), bf16[8,32,128]{2,1,0:T(8,128)(2,1)S(1)}, u32[]{:S(2)}, u32[]{:S(2)}) %all-to-all-start.5) | async-done | bytes 65568 | tf_op jit(solution)/shard_map/all_to_all | solution.py:152
  702.1 4.8 all-to-all-start.4
  706.9 0.6 copy_bitcast_fusion.4
  707.5 0.6 copy_bitcast_fusion.5
  708.2 8.3 %all-to-all-done.4 = bf16[8,32,640]{2,1,0:T(8,128)(2,1)S(1)} async-done(((bf16[8,32,640]{2,1,0:T(8,128)(2,1)}), bf16[8,32,640]{2,1,0:T(8,128)(2,1)S(1)}, u32[]{:S(2)}, u32[]{:S(2)}) %all-to-all-start.4) | async-done | bytes 327712 | tf_op jit(solution)/shard_map/all_to_all | solution.py:151
  716.4 0.8 copy.107
  (57 shorter events, 3.1 us)
Async XLA Ops:
  7.2 0.8 copy-start
  7.2 45.3 %copy-start.1 = (s32[128]{0:T(128)S(1)}, s32[128]{0:T(128)}, u32[]{:S(2)}) copy-start(s32[128]{0:T(128)} %param.16) | copy-start | bytes 1540
  8.0 48.4 %copy-start.2 = (bf16[32,5120]{1,0:T(8,128)(2,1)S(1)}, bf16[32,5120]{1,0:T(8,128)(2,1)}, u32[]{:S(2)}) copy-start(bf16[32,5120]{1,0:T(8,128)(2,1)} %param.15) | copy-start | bytes 983044
  8.7 22.1 %all-to-all-start = ((bf16[32,8,128]{2,0,1:T(8,128)(2,1)}), bf16[32,8,128]{2,0,1:T(8,128)(2,1)S(1)}, u32[]{:S(2)}, u32[]{:S(2)}) async-start(bf16[32,8,128]{2,0,1:T(8,128)(2,1)} %copy_bitcast_fusion.7), calls=%async_computation | async-start | bytes 131072 | tf_op jit(solution)/shard_map/all_to_all | solution.py:69
  30.7 13.6 %all-to-all-start.1 = ((bf16[32,8,128]{2,0,1:T(8,128)(2,1)}), bf16[32,8,128]{2,0,1:T(8,128)(2,1)S(1)}, u32[]{:S(2)}, u32[]{:S(2)}) async-start(bf16[32,8,128]{2,0,1:T(8,128)(2,1)} %copy_bitcast_fusion.6), calls=%async_computation.1 | async-start | bytes 131072 | tf_op jit(solution)/shard_map/all_to_all | solution.py:70
  35.5 133.3 %all-gather.3.cloned.1.call-start = ((), (), s32[]{:S(2)}) async-start(), calls=%async_computation.8 | async-start | bytes 4259840 | tf_op jit(solution)/shard_map/all_gather | solution.py:16
  46.7 14.4 %all-to-all-start.2 = ((bf16[32,8,640]{2,0,1:T(8,128)(2,1)}), bf16[32,8,640]{2,0,1:T(8,128)(2,1)S(1)}, u32[]{:S(2)}, u32[]{:S(2)}) async-start(bf16[32,8,640]{2,0,1:T(8,128)(2,1)} %bitcast.236), calls=%async_computation.2 | async-start | bytes 655360 | tf_op jit(solution)/shard_map/all_to_all | solution.py:68
  61.1 19.8 %all-to-all-start.3 = ((bf16[32,8,640]{2,0,1:T(8,128)(2,1)}), bf16[32,8,640]{2,0,1:T(8,128)(2,1)S(1)}, u32[]{:S(2)}, u32[]{:S(2)}) async-start(bf16[32,8,640]{2,0,1:T(8,128)(2,1)} %bitcast.235), calls=%async_computation.3 | async-start | bytes 655360 | tf_op jit(solution)/shard_map/all_to_all | solution.py:71
  67.4 600.4 %all-reduce.2.cloned.1.call-start = ((), (), s32[]{:S(2)}) async-start(), calls=%async_computation.7 | async-start | bytes 262144 | tf_op jit(solution)/shard_map/psum | solution.py:141
  67.5 104.0 %collective-permute-start = (bf16[2,128,256]{2,1,0:T(8,128)(2,1)S(1)}, bf16[2,128,256]{2,1,0:T(8,128)(2,1)S(1)}, u32[]{:S(2)}, u32[]{:S(2)}) collective-permute-start(bf16[2,128,256]{2,1,0:T(8,128)(2,1)S(1)} %pad_maximum_fusion.1), channel_id=1, source_target_pairs={{0,16},{8,24},{16,32},{24,40},{32,48},{40,56},{48,64},{56,72},{64,... | collective-permute-start | bytes 393224 | tf_op jit(solution)/shard_map/ppermute | solution.py:22
  70.9 100.6 %collective-permute-start.1 = (bf16[2,128,256]{2,1,0:T(8,128)(2,1)S(1)}, bf16[2,128,256]{2,1,0:T(8,128)(2,1)S(1)}, u32[]{:S(2)}, u32[]{:S(2)}) collective-permute-start(bf16[2,128,256]{2,1,0:T(8,128)(2,1)S(1)} %pad_maximum_fusion.1), channel_id=1, source_target_pairs={{0,8},{8,16},{16,24},{24,32},{32,40},{40,48},{48,56},{56,64},{64,7... | collective-permute-start | bytes 393224 | tf_op jit(solution)/shard_map/ppermute | solution.py:22
  184.7 3.9 collective-permute-start.2
  186.0 12.5 %collective-permute-start.3 = (f32[2,128,256]{2,1,0:T(8,128)S(1)}, f32[2,128,256]{2,1,0:T(8,128)}, u32[]{:S(2)}, u32[]{:S(2)}) collective-permute-start(f32[2,128,256]{2,1,0:T(8,128)S(1)} %bitcast.271), channel_id=1, source_target_pairs={{16,0},{24,8},{32,16},{40,24},{48,32},{56,40},{64,48},{72,56},{80,... | collective-permute-start | bytes 786440 | tf_op jit(solution)/shard_map/ppermute | solution.py:22
  669.4 19.1 %all-to-all-start.6 = ((bf16[8,32,128]{2,1,0:T(8,128)(2,1)}), bf16[8,32,128]{2,1,0:T(8,128)(2,1)S(1)}, u32[]{:S(2)}, u32[]{:S(2)}) async-start(bf16[8,32,128]{2,1,0:T(8,128)(2,1)} %bitcast.70), calls=%async_computation.6 | async-start | bytes 131072 | tf_op jit(solution)/shard_map/all_to_all | solution.py:153
  688.6 13.6 %all-to-all-start.5 = ((bf16[8,32,128]{2,1,0:T(8,128)(2,1)}), bf16[8,32,128]{2,1,0:T(8,128)(2,1)S(1)}, u32[]{:S(2)}, u32[]{:S(2)}) async-start(bf16[8,32,128]{2,1,0:T(8,128)(2,1)} %bitcast.68), calls=%async_computation.5 | async-start | bytes 131072 | tf_op jit(solution)/shard_map/all_to_all | solution.py:152
  702.1 14.3 %all-to-all-start.4 = ((bf16[8,32,640]{2,1,0:T(8,128)(2,1)}), bf16[8,32,640]{2,1,0:T(8,128)(2,1)S(1)}, u32[]{:S(2)}, u32[]{:S(2)}) async-start(bf16[8,32,640]{2,1,0:T(8,128)(2,1)} %bitcast.44), calls=%async_computation.4 | async-start | bytes 655360 | tf_op jit(solution)/shard_map/all_to_all | solution.py:151
Sparse Core Ops, SparseCore 0:
  45.1 123.6 all-gather.2
  188.6 479.1 all-reduce.1
